TPU v7x, 32 devices: a whole 2x2x4 slice. The times are simulated.
32 devices in a mesh: energy: 4 (over z), atom: 8 (over y, x, core).
Axes of the slice: x: 2, y: 2, z: 4, core: 2. Of those that a mesh axis runs over, the one named last changes fastest.
Arguments:
- t_mats: bfloat16 [4, 16, 2048], P('energy', 'atom'), may hold values from -0.75 to 0.75
- struct_table: bfloat16 [4, 64, 2048], P('energy'), may hold values from -0.359375 to 0.359375
- zone_atoms: int32 [16, 64], P('atom'), may hold values from 0 to 15, as said below
- zone_size: int32 [16], P('atom'), may hold values from 32 to 64
- pair_index: int32 [16, 384], P('atom'), may hold values from 0 to 63
- zone_link: int32 [16, 384], P('atom'), may hold values from 0 to 63
- weights: float32 [4, 2], P('energy'), may hold values from -1 to 1
Outputs:
- green: float32 [16, 2048], P('atom')
Inputs may be any that keep to these rules, and one draw needn't show every extreme that they name: Atom g is owned by index g // 2 of the atom axis; zone_atoms[g, 0] is g; the owner of every member of atom g's zone lies -4 to 3 steps from g's owner along the atom axis, counted around the axis, and both extreme offsets occur in every zone; members may repeat (periodic images).
All inputs are finite; a program needn't handle non-finite values.
Results may differ from a plain program's by a relative error of at most 0.003.
Values may be sent and summed in bfloat16 or wider, within the bound.
No kernel may reach another device: no remote copies, remote signals or barrier semaphores. Data moves between devices by JAX's collectives and lax.ppermute only.
A program may use at most 128 MiB of HBM per device.

v0:
```python
import functools

import jax
import jax.numpy as jnp
from jax import lax
from jax.experimental import pallas as pl
from jax.experimental.pallas import tpu as pltpu
from jax.sharding import PartitionSpec as P

L = 32
Z = 64
NB = 6


def real_form(block):
    parts = block.reshape(block.shape[:-1] + (2, L, L))
    real_part = parts[..., 0, :, :]
    imag_part = parts[..., 1, :, :]
    top_rows = jnp.concatenate([real_part, -imag_part], axis=-1)
    bottom_rows = jnp.concatenate([imag_part, real_part], axis=-1)
    return jnp.concatenate([top_rows, bottom_rows], axis=-2)


def zone_kernel(links, pairs, atoms, sizes, wts, reach, tab, tw, out, q, near3, acc, acc2, lists):
    a_dev = out.shape[0]
    zl = L * 2
    n1 = NB * NB
    width = 4
    spare = NB

    def rows(index):
        return pl.ds(pl.multiple_of(index * zl, zl), zl)

    def dot(a, b):
        return jnp.dot(a, b, preferred_element_type=jnp.float32)

    zero_b = jnp.zeros((zl, L), jnp.bfloat16)
    zero_f = jnp.zeros((zl, L), jnp.float32)
    for g in range(a_dev):
        size = sizes[g]
        own = atoms[g, 0]
        start_b = tw[rows(own), :][:, :L]
        start_f = start_b.astype(jnp.float32)
        q[...] = dot(tab[...], start_b)

        for j in range(lists.shape[1]):
            lists[0, j] = jnp.int32(0)
            lists[1, j] = jnp.int32(0)
            lists[2, j] = jnp.int32(spare)
        count = jnp.int32(0)
        for m in range(NB):
            base = links[g, m] * NB
            for n in range(NB):
                slot = links[g, base + n]
                lists[0, count] = slot
                lists[1, count] = pairs[g, base + n]
                lists[2, count] = jnp.int32(m)
                count = count + jnp.logical_or(reach[g, slot] != 0, slot == 0).astype(jnp.int32)
            lists[3, m] = jnp.int32(0)
        acc2[...] = jnp.zeros(acc2.shape, jnp.float32)

        def sweep1(c, carry):
            parts = []
            for u in range(width):
                j = c * width + u
                slot = lists[0, j]
                coupled = zero_f
                for k in range(NB):
                    spot = slot * NB + k
                    coupled = coupled + jnp.where(links[g, spot] == 0, q[rows(pairs[g, spot]), :], 0.0)
                col = jnp.where(slot < size, dot(tw[rows(atoms[g, slot]), :], coupled.astype(jnp.bfloat16)), 0.0)
                col = col + jnp.where(slot == 0, start_f, 0.0)
                parts.append(dot(tab[rows(lists[1, j]), :], col.astype(jnp.bfloat16)))
            for u in range(width):
                j = c * width + u
                m = lists[2, j]
                acc2[m] += parts[u]
                lists[3, m] = jnp.int32(1)
            return carry

        lax.fori_loop(0, (count + width - 1) // width, sweep1, 0)

        for m in range(NB):
            slot = links[g, m]
            live = jnp.logical_and(lists[3, m] != 0, slot < size)

            @pl.when(live)
            def _():
                col = dot(tw[rows(atoms[g, slot]), :], acc2[m].astype(jnp.bfloat16))
                col = col + jnp.where(slot == 0, start_f, 0.0)
                near3[rows(m), :] = col.astype(jnp.bfloat16)

            @pl.when(jnp.logical_not(live))
            def _():
                near3[rows(m), :] = jnp.where(slot == 0, start_b, zero_b)

        acc[...] = zero_f
        for n in range(NB):
            acc[...] += dot(tab[rows(pairs[g, n]), :], near3[rows(n), :])
        col = dot(tw[rows(own), :], acc[...].astype(jnp.bfloat16)) + start_f
        w_real = wts[0, 0]
        w_imag = wts[0, 1]
        out[g, :L, :] = w_real * col[:L] - w_imag * col[L:]
        out[g, L:, :] = w_real * col[L:] + w_imag * col[:L]


def xor_pairs(n, bit):
    return [(i, i ^ bit) for i in range(n)]


def gather_atoms(t_mats, n_axis, later):
    if n_axis & (n_axis - 1):
        return lax.all_gather(t_mats, "atom", axis=1, tiled=True), later
    index = lax.axis_index("atom")
    blocks = t_mats
    bit = 1
    while bit < n_axis:
        other = lax.ppermute(blocks, "atom", xor_pairs(n_axis, bit))
        if bit <= 2:
            other, later[bit - 1] = lax.optimization_barrier((other, later[bit - 1]))
        low = (index & bit) == 0
        blocks = jnp.where(
            low, jnp.concatenate([blocks, other], axis=1), jnp.concatenate([other, blocks], axis=1)
        )
        bit *= 2
    return blocks, later


def sum_energies(x, n_axis):
    if n_axis & (n_axis - 1):
        return lax.psum(x, "energy")
    bit = 1
    while bit < n_axis:
        x = x + lax.ppermute(x, "energy", xor_pairs(n_axis, bit))
        bit *= 2
    return x


def body(axis_sizes, t_mats, struct_table, zone_atoms, zone_size, pair_index, zone_link, weights):
    e_dev, a_dev, block_flat = t_mats.shape
    window, (table, zone_link) = gather_atoms(t_mats, axis_sizes["atom"], [struct_table, zone_link])
    n_atoms = window.shape[1]
    k_tab = struct_table.shape[1]
    tab = real_form(table[0]).reshape(k_tab * 2 * L, 2 * L)
    tw = real_form(window[0]).reshape(n_atoms * 2 * L, 2 * L)
    z_slots = zone_atoms.shape[1]
    reach = jnp.any(zone_link.reshape(a_dev, z_slots, NB) == 0, axis=-1).astype(jnp.int32)
    smem = pl.BlockSpec(memory_space=pltpu.SMEM)
    vmem = pl.BlockSpec(memory_space=pltpu.VMEM)
    blocks = pl.pallas_call(
        zone_kernel,
        out_shape=jax.ShapeDtypeStruct((a_dev, 2 * L, L), jnp.float32),
        in_specs=[smem, smem, smem, smem, smem, smem, vmem, vmem],
        out_specs=vmem,
        scratch_shapes=[
            pltpu.VMEM((k_tab * 2 * L, L), jnp.float32),
            pltpu.VMEM((NB * 2 * L, L), jnp.bfloat16),
            pltpu.VMEM((2 * L, L), jnp.float32),
            pltpu.VMEM((NB + 1, 2 * L, L), jnp.float32),
            pltpu.SMEM((4, NB * NB + 4), jnp.int32),
        ],
    )(zone_link, pair_index, zone_atoms, zone_size, weights, reach, tab, tw)
    blocks = sum_energies(blocks, axis_sizes["energy"])
    return blocks.reshape(a_dev, 2, L * L).reshape(a_dev, 2 * L * L)


def solution(mesh):
    return jax.shard_map(
        functools.partial(body, dict(mesh.shape)),
        mesh=mesh,
        in_specs=(
            P("energy", "atom", None),
            P("energy", None, None),
            P("atom", None),
            P("atom"),
            P("atom", None),
            P("atom", None),
            P("energy", None),
        ),
        out_specs=P("atom", None),
        check_vma=False,
    )
```

profile of v0, /device:TPU:6, one launch (start us, length us, event | category | flops | bytes accessed | tf_op | source)
XLA Modules:
  0.0 30.7 jit_solution(10096978310445279644)
XLA Ops:
  0.0 0.0 collective-permute-start
  0.0 0.8 %concatenate.135 = bf16[2,2,32,32]{3,2,1,0:T(8,128)(2,1)S(1)} reshape(bf16[1,2,2048]{2,1,0:T(2,128)(2,1)} %param.7) | data formatting | bytes 16384 | tf_op jit(solution)/shard_map/concatenate | solution.py:123
  0.8 0.0 copy-start
  0.8 0.6 %collective-permute-done = bf16[1,2,2048]{2,1,0:T(2,128)(2,1)S(1)} collective-permute-done((bf16[1,2,2048]{2,1,0:T(2,128)(2,1)}, bf16[1,2,2048]{2,1,0:T(2,128)(2,1)S(1)}, u32[]{:S(2)}, u32[]{:S(2)}) %collective-permute-start) | collective-permute-done | bytes 8224 | tf_op jit(solution)/shard_map/ppermute | solution.py:118
  1.4 1.2 %copy.18 = bf16[1,64,2048]{1,2,0:T(8,128)(2,1)S(1)} copy(bf16[1,64,2048]{2,1,0:T(8,128)(2,1)} %param.8) | data formatting | bytes 524288 | tf_op jit(solution)/shard_map/optimization_barrier | solution.py:120
  2.7 0.1 concatenate.136
  2.8 0.0 copy-done
  2.8 0.6 %collective-permute-start.1 = (bf16[1,4,2048]{2,1,0:T(4,128)(2,1)S(1)}, bf16[1,4,2048]{2,1,0:T(4,128)(2,1)S(1)}, u32[]{:S(2)}, u32[]{:S(2)}) collective-permute-start(bf16[1,4,2048]{2,1,0:T(4,128)(2,1)S(1)} %maximum_select_fusion.3), channel_id=1, source_target_pairs={{0,2},{1,3},{2,0},{3,1},{4,6},{5,7},{6,4},{7,5},{8,10},{9,11},{10,... | collective-permute-start | bytes 49160 | tf_op jit(solution)/shard_map/ppermute | solution.py:118
  3.5 0.3 maximum_maximum_fusion
  3.8 0.0 copy-start.1
  3.8 2.4 %copy.19 = bf16[64,64,64]{2,1,0:T(8,128)(2,1)} copy(bf16[64,64,64]{0,2,1:T(8,128)(2,1)S(1)} %maximum_maximum_fusion) | data formatting | bytes 1048576 | tf_op jit(solution)/shard_map/concatenate | solution.py:21
  6.2 0.4 %collective-permute-done.1 = bf16[1,4,2048]{2,1,0:T(4,128)(2,1)S(1)} collective-permute-done((bf16[1,4,2048]{2,1,0:T(4,128)(2,1)S(1)}, bf16[1,4,2048]{2,1,0:T(4,128)(2,1)S(1)}, u32[]{:S(2)}, u32[]{:S(2)}) %collective-permute-start.1) | collective-permute-done | bytes 16416 | tf_op jit(solution)/shard_map/ppermute | solution.py:118
  6.7 0.1 concatenate.139
  6.8 0.6 %collective-permute-start.2 = (bf16[1,8,2048]{2,1,0:T(8,128)(2,1)S(1)}, bf16[1,8,2048]{2,1,0:T(8,128)(2,1)S(1)}, u32[]{:S(2)}, u32[]{:S(2)}) collective-permute-start(bf16[1,8,2048]{2,1,0:T(8,128)(2,1)S(1)} %maximum_select_fusion.2), channel_id=1, source_target_pairs={{0,4},{1,5},{2,6},{3,7},{4,0},{5,1},{6,2},{7,3},{8,12},{9,13},{10,... | collective-permute-start | bytes 98312 | tf_op jit(solution)/shard_map/ppermute | solution.py:118
  7.4 0.0 copy-done.1
  7.4 0.2 eq.21
  7.6 0.1 reduce_or.9
  7.7 0.6 %convert_element_type.3.reach = s32[2,64]{1,0:T(2,128)} convert(pred[2,64]{1,0:T(4,128)(4,1)S(1)} %reduce_or.9) | non-fusion elementwise | flops 128 | bytes 640 | tf_op jit(solution)/shard_map/convert_element_type | solution.py:147
  8.3 2.5 %collective-permute-done.2 = bf16[1,8,2048]{2,1,0:T(8,128)(2,1)S(1)} collective-permute-done((bf16[1,8,2048]{2,1,0:T(8,128)(2,1)S(1)}, bf16[1,8,2048]{2,1,0:T(8,128)(2,1)S(1)}, u32[]{:S(2)}, u32[]{:S(2)}) %collective-permute-start.2) | collective-permute-done | bytes 32800 | tf_op jit(solution)/shard_map/ppermute | solution.py:118
  10.8 0.1 concatenate.149
  10.9 0.1 maximum_select_fusion
  11.1 0.9 %maximum_maximum_fusion.1 = bf16[16,64,64]{2,1,0:T(8,128)(2,1)} fusion(bf16[16,32,32]{2,1,0:T(8,128)(2,1)S(1)} %get-tuple-element.16, bf16[16,32,32]{2,1,0:T(8,128)(2,1)S(1)} %get-tuple-element.15, bf16[16,32,32]{2,1,0:T(8,128)(2,1)S(1)} %fusion.1), kind=kLoop, calls=%fused_computation.4 | loop fusion | flops 524288 | bytes 229376 | tf_op jit(solution)/shard_map/concatenate | solution.py:21
  11.9 6.1 %shard_map.73 = f32[2,64,32]{2,1,0:T(8,128)} custom-call(s32[2,384]{1,0:T(2,128)} %links, s32[2,384]{1,0:T(2,128)} %pairs.1, s32[2,64]{1,0:T(2,128)} %atoms.1, s32[2]{0:T(128)} %sizes.1, f32[1,2]{1,0:T(1,128)} %wts.1, s32[2,64]{1,0:T(2,128)} %convert_element_type.3.reach, bf16[4096,64]{1,0:T(8,128)(2,1)} %bitcast.19, bf16[1024,64]{1,0:T(8,128)(2,1)} %bitcast.22), custom_call_target="tpu_custom_call" | custom-call | tf_op jit(solution)/shard_map/pallas_call | solution.py:150
  18.0 1.6 %collective-permute-start.3 = (f32[2,64,32]{2,1,0:T(8,128)}, f32[2,64,32]{2,1,0:T(8,128)S(1)}, u32[]{:S(2)}, u32[]{:S(2)}) collective-permute-start(f32[2,64,32]{2,1,0:T(8,128)} %shard_map.73), channel_id=1, source_target_pairs={{0,8},{8,0},{16,24},{24,16},{1,9},{9,1},{17,25},{25,17},{2,10},{10... | collective-permute-start | bytes 49160 | tf_op jit(solution)/shard_map/ppermute | solution.py:134
  19.6 3.6 %collective-permute-done.3 = f32[2,64,32]{2,1,0:T(8,128)S(1)} collective-permute-done((f32[2,64,32]{2,1,0:T(8,128)}, f32[2,64,32]{2,1,0:T(8,128)S(1)}, u32[]{:S(2)}, u32[]{:S(2)}) %collective-permute-start.3) | collective-permute-done | bytes 16416 | tf_op jit(solution)/shard_map/ppermute | solution.py:134
  23.2 0.9 %add.6 = f32[2,64,32]{2,1,0:T(8,128)S(1)} add(f32[2,64,32]{2,1,0:T(8,128)} %shard_map.73, f32[2,64,32]{2,1,0:T(8,128)S(1)} %collective-permute-done.3) | non-fusion elementwise | flops 4096 | bytes 49152 | tf_op jit(solution)/shard_map/add | solution.py:134
  24.1 2.1 %collective-permute-start.4 = (f32[2,64,32]{2,1,0:T(8,128)S(1)}, f32[2,64,32]{2,1,0:T(8,128)S(1)}, u32[]{:S(2)}, u32[]{:S(2)}) collective-permute-start(f32[2,64,32]{2,1,0:T(8,128)S(1)} %add.6), channel_id=1, source_target_pairs={{0,16},{8,24},{16,0},{24,8},{1,17},{9,25},{17,1},{25,9},{2,18},{10... | collective-permute-start | bytes 49160 | tf_op jit(solution)/shard_map/ppermute | solution.py:134
  26.2 3.8 %collective-permute-done.4 = f32[2,64,32]{2,1,0:T(8,128)S(1)} collective-permute-done((f32[2,64,32]{2,1,0:T(8,128)S(1)}, f32[2,64,32]{2,1,0:T(8,128)S(1)}, u32[]{:S(2)}, u32[]{:S(2)}) %collective-permute-start.4) | collective-permute-done | bytes 16416 | tf_op jit(solution)/shard_map/ppermute | solution.py:134
  30.0 0.7 %reshape_reshape.3 = f32[2,2048]{1,0:T(2,128)} reshape(f32[2,64,32]{2,1,0:T(8,128)S(1)} %add.7) | data formatting | bytes 32768 | tf_op jit(solution)/shard_map/reshape;reshape | solution.py:164
  (12 shorter events, 0.3 us)
Async XLA Ops:
  0.0 1.4 %collective-permute-start = (bf16[1,2,2048]{2,1,0:T(2,128)(2,1)}, bf16[1,2,2048]{2,1,0:T(2,128)(2,1)S(1)}, u32[]{:S(2)}, u32[]{:S(2)}) collective-permute-start(bf16[1,2,2048]{2,1,0:T(2,128)(2,1)} %param.7), channel_id=1, source_target_pairs={{0,1},{1,0},{2,3},{3,2},{4,5},{5,4},{6,7},{7,6},{8,9},{9,8},{10,11... | collective-permute-start | bytes 24584 | tf_op jit(solution)/shard_map/ppermute | solution.py:118
  0.8 2.0 %copy-start = (bf16[1,2,2048]{2,1,0:T(2,128)(2,1)S(1)}, bf16[1,2,2048]{2,1,0:T(2,128)(2,1)}, u32[]{:S(2)}) copy-start(bf16[1,2,2048]{2,1,0:T(2,128)(2,1)} %param.7) | copy-start | bytes 24580
  2.8 3.8 %collective-permute-start.1 = (bf16[1,4,2048]{2,1,0:T(4,128)(2,1)S(1)}, bf16[1,4,2048]{2,1,0:T(4,128)(2,1)S(1)}, u32[]{:S(2)}, u32[]{:S(2)}) collective-permute-start(bf16[1,4,2048]{2,1,0:T(4,128)(2,1)S(1)} %maximum_select_fusion.3), channel_id=1, source_target_pairs={{0,2},{1,3},{2,0},{3,1},{4,6},{5,7},{6,4},{7,5},{8,10},{9,11},{10,... | collective-permute-start | bytes 49160 | tf_op jit(solution)/shard_map/ppermute | solution.py:118
  3.8 3.6 %copy-start.1 = (s32[2,384]{1,0:T(2,128)S(1)}, s32[2,384]{1,0:T(2,128)}, u32[]{:S(2)}) copy-start(s32[2,384]{1,0:T(2,128)} %links) | copy-start | bytes 9220
  6.8 4.0 %collective-permute-start.2 = (bf16[1,8,2048]{2,1,0:T(8,128)(2,1)S(1)}, bf16[1,8,2048]{2,1,0:T(8,128)(2,1)S(1)}, u32[]{:S(2)}, u32[]{:S(2)}) collective-permute-start(bf16[1,8,2048]{2,1,0:T(8,128)(2,1)S(1)} %maximum_select_fusion.2), channel_id=1, source_target_pairs={{0,4},{1,5},{2,6},{3,7},{4,0},{5,1},{6,2},{7,3},{8,12},{9,13},{10,... | collective-permute-start | bytes 98312 | tf_op jit(solution)/shard_map/ppermute | solution.py:118
  18.0 5.2 %collective-permute-start.3 = (f32[2,64,32]{2,1,0:T(8,128)}, f32[2,64,32]{2,1,0:T(8,128)S(1)}, u32[]{:S(2)}, u32[]{:S(2)}) collective-permute-start(f32[2,64,32]{2,1,0:T(8,128)} %shard_map.73), channel_id=1, source_target_pairs={{0,8},{8,0},{16,24},{24,16},{1,9},{9,1},{17,25},{25,17},{2,10},{10... | collective-permute-start | bytes 49160 | tf_op jit(solution)/shard_map/ppermute | solution.py:134
  24.1 5.9 %collective-permute-start.4 = (f32[2,64,32]{2,1,0:T(8,128)S(1)}, f32[2,64,32]{2,1,0:T(8,128)S(1)}, u32[]{:S(2)}, u32[]{:S(2)}) collective-permute-start(f32[2,64,32]{2,1,0:T(8,128)S(1)} %add.6), channel_id=1, source_target_pairs={{0,16},{8,24},{16,0},{24,8},{1,17},{9,25},{17,1},{25,9},{2,18},{10... | collective-permute-start | bytes 49160 | tf_op jit(solution)/shard_map/ppermute | solution.py:134
where the time goes:
time: 30.5 us; the launch traced here: 30.7 us
  waiting for transfers between devices  10.9 us (36%)
  Pallas kernels  6.09 us (20%)
  local copies, waits for them, and re-layouts  5.63 us (18%)
  starting transfers between devices  4.87 us (16%)
  other arithmetic  3.01 us (10%)
    ppermute x2, waiting for transfers between devices, sum_energies(): x = x + lax.ppermute(x, 'energy', xor_pairs(n_axis, bit))  7.41 us
    pallas_call x1, Pallas kernels, body(): pl.pallas_call(zone_kernel, out_shape=jax.ShapeDtypeStruct((a_dev, 2 * L,...  6.09 us
    ppermute x2, starting transfers between devices, sum_energies(): x = x + lax.ppermute(x, 'energy', xor_pairs(n_axis, bit))  3.69 us
    ppermute x3, waiting for transfers between devices, gather_atoms(): other = lax.ppermute(blocks, 'atom', xor_pairs(n_axis, bit))  3.51 us
    concatenate x1, local copies, waits for them, and re-layouts, real_form(): return jnp.concatenate([top_rows, bottom_rows], axis=-2)  2.36 us
    optimization_barrier x1, local copies, waits for them, and re-layouts, gather_atoms(): other, later[bit - 1] = lax.optimization_barrier((other, later[bit - 1]))  1.22 us
    ppermute x3, starting transfers between devices, gather_atoms(): other = lax.ppermute(blocks, 'atom', xor_pairs(n_axis, bit))  1.17 us
    concatenate x2, other arithmetic, real_form(): return jnp.concatenate([top_rows, bottom_rows], axis=-2)  1.15 us
  transfers between devices with their start and end apart: 5, of which 5 were waited for; matrix products, arithmetic and copies ran while one was open for 14% of the time, Pallas kernels for 0%

commit v1 on v0

--- a/solution.py
+++ b/solution.py
@@ -100,8 +100,10 @@
         col = dot(tw[rows(own), :], acc[...].astype(jnp.bfloat16)) + start_f
         w_real = wts[0, 0]
         w_imag = wts[0, 1]
-        out[g, :L, :] = w_real * col[:L] - w_imag * col[L:]
-        out[g, L:, :] = w_real * col[L:] + w_imag * col[:L]
+        green = jnp.concatenate(
+            [w_real * col[:L] - w_imag * col[L:], w_real * col[L:] + w_imag * col[:L]], axis=0
+        )
+        out[g] = green.reshape(out.shape[1:])
 
 
 def xor_pairs(n, bit):
@@ -149,7 +151,7 @@
     vmem = pl.BlockSpec(memory_space=pltpu.VMEM)
     blocks = pl.pallas_call(
         zone_kernel,
-        out_shape=jax.ShapeDtypeStruct((a_dev, 2 * L, L), jnp.float32),
+        out_shape=jax.ShapeDtypeStruct((a_dev, 2 * L * L // 128, 128), jnp.float32),
         in_specs=[smem, smem, smem, smem, smem, smem, vmem, vmem],
         out_specs=vmem,
         scratch_shapes=[
@@ -161,7 +163,7 @@
         ],
     )(zone_link, pair_index, zone_atoms, zone_size, weights, reach, tab, tw)
     blocks = sum_energies(blocks, axis_sizes["energy"])
-    return blocks.reshape(a_dev, 2, L * L).reshape(a_dev, 2 * L * L)
+    return blocks.reshape(a_dev, 2 * L * L)
 
 
 def solution(mesh):

time: 30.5 us -> 29.2 us (0.957)
  the two profiles are of different devices: /device:TPU:6 before, /device:TPU:0 now
where the time goes in v1:
time: 29.2 us; the launch traced here: 29.1 us
  starting transfers between devices  9.1 us (31%)
  waiting for transfers between devices  6.12 us (21%)
  local copies, waits for them, and re-layouts  5.55 us (19%)
  Pallas kernels  5.27 us (18%)
  other arithmetic  2.88 us (10%)
    pallas_call x1, Pallas kernels, body(): pl.pallas_call(zone_kernel, out_shape=jax.ShapeDtypeStruct((a_dev, 2 * L...  5.27 us
    ppermute x3, starting transfers between devices, gather_atoms(): other = lax.ppermute(blocks, 'atom', xor_pairs(n_axis, bit))  4.93 us
    ppermute x2, waiting for transfers between devices, sum_energies(): x = x + lax.ppermute(x, 'energy', xor_pairs(n_axis, bit))  4.42 us
    ppermute x2, starting transfers between devices, sum_energies(): x = x + lax.ppermute(x, 'energy', xor_pairs(n_axis, bit))  4.16 us
    concatenate x1, local copies, waits for them, and re-layouts, real_form(): return jnp.concatenate([top_rows, bottom_rows], axis=-2)  2.36 us
    ppermute x3, waiting for transfers between devices, gather_atoms(): other = lax.ppermute(blocks, 'atom', xor_pairs(n_axis, bit))  1.7 us
    optimization_barrier x1, local copies, waits for them, and re-layouts, gather_atoms(): other, later[bit - 1] = lax.optimization_barrier((other, later[bit - 1]))  1.22 us
    concatenate x2, other arithmetic, real_form(): return jnp.concatenate([top_rows, bottom_rows], axis=-2)  1.15 us
  transfers between devices with their start and end apart: 5, of which 4 were waited for; matrix products, arithmetic and copies ran while one was open for 15% of the time, Pallas kernels for 0%

profile of v1, /device:TPU:0, one launch (start us, length us, event | category | flops | bytes accessed | tf_op | source)
XLA Modules:
  0.0 29.1 jit_solution(3271113349134493572)
XLA Ops:
  0.0 0.5 %collective-permute-start = (bf16[1,2,2048]{2,1,0:T(2,128)(2,1)}, bf16[1,2,2048]{2,1,0:T(2,128)(2,1)S(1)}, u32[]{:S(2)}, u32[]{:S(2)}) collective-permute-start(bf16[1,2,2048]{2,1,0:T(2,128)(2,1)} %param.7), channel_id=1, source_target_pairs={{0,1},{1,0},{2,3},{3,2},{4,5},{5,4},{6,7},{7,6},{8,9},{9,8},{10,11... | collective-permute-start | bytes 24584 | tf_op jit(solution)/shard_map/ppermute | solution.py:120
  0.5 0.8 %concatenate.135 = bf16[2,2,32,32]{3,2,1,0:T(8,128)(2,1)S(1)} reshape(bf16[1,2,2048]{2,1,0:T(2,128)(2,1)} %param.7) | data formatting | bytes 16384 | tf_op jit(solution)/shard_map/concatenate | solution.py:125
  1.3 0.0 copy-start
  1.3 0.2 collective-permute-done
  1.5 1.2 %copy.18 = bf16[1,64,2048]{1,2,0:T(8,128)(2,1)S(1)} copy(bf16[1,64,2048]{2,1,0:T(8,128)(2,1)} %param.8) | data formatting | bytes 524288 | tf_op jit(solution)/shard_map/optimization_barrier | solution.py:122
  2.8 0.1 concatenate.136
  2.9 0.0 copy-done
  3.0 2.9 %collective-permute-start.1 = (bf16[1,4,2048]{2,1,0:T(4,128)(2,1)S(1)}, bf16[1,4,2048]{2,1,0:T(4,128)(2,1)S(1)}, u32[]{:S(2)}, u32[]{:S(2)}) collective-permute-start(bf16[1,4,2048]{2,1,0:T(4,128)(2,1)S(1)} %maximum_select_fusion.3), channel_id=1, source_target_pairs={{0,2},{1,3},{2,0},{3,1},{4,6},{5,7},{6,4},{7,5},{8,10},{9,11},{10,... | collective-permute-start | bytes 49160 | tf_op jit(solution)/shard_map/ppermute | solution.py:120
  5.9 0.3 maximum_maximum_fusion
  6.2 0.0 copy-start.1
  6.2 2.4 %copy.19 = bf16[64,64,64]{2,1,0:T(8,128)(2,1)} copy(bf16[64,64,64]{0,2,1:T(8,128)(2,1)S(1)} %maximum_maximum_fusion) | data formatting | bytes 1048576 | tf_op jit(solution)/shard_map/concatenate | solution.py:21
  8.6 0.0 collective-permute-done.1
  8.6 0.1 concatenate.139
  8.8 1.6 %collective-permute-start.2 = (bf16[1,8,2048]{2,1,0:T(8,128)(2,1)S(1)}, bf16[1,8,2048]{2,1,0:T(8,128)(2,1)S(1)}, u32[]{:S(2)}, u32[]{:S(2)}) collective-permute-start(bf16[1,8,2048]{2,1,0:T(8,128)(2,1)S(1)} %maximum_select_fusion.2), channel_id=1, source_target_pairs={{0,4},{1,5},{2,6},{3,7},{4,0},{5,1},{6,2},{7,3},{8,12},{9,13},{10,... | collective-permute-start | bytes 98312 | tf_op jit(solution)/shard_map/ppermute | solution.py:120
  10.4 0.0 copy-done.1
  10.4 0.2 eq.21
  10.6 0.1 reduce_or.9
  10.7 0.6 %convert_element_type.3.reach = s32[2,64]{1,0:T(2,128)} convert(pred[2,64]{1,0:T(4,128)(4,1)S(1)} %reduce_or.9) | non-fusion elementwise | flops 128 | bytes 640 | tf_op jit(solution)/shard_map/convert_element_type | solution.py:149
  11.3 1.5 %collective-permute-done.2 = bf16[1,8,2048]{2,1,0:T(8,128)(2,1)S(1)} collective-permute-done((bf16[1,8,2048]{2,1,0:T(8,128)(2,1)S(1)}, bf16[1,8,2048]{2,1,0:T(8,128)(2,1)S(1)}, u32[]{:S(2)}, u32[]{:S(2)}) %collective-permute-start.2) | collective-permute-done | bytes 32800 | tf_op jit(solution)/shard_map/ppermute | solution.py:120
  12.7 0.1 concatenate.149
  12.9 0.1 maximum_select_fusion
  13.0 0.9 %maximum_maximum_fusion.1 = bf16[16,64,64]{2,1,0:T(8,128)(2,1)} fusion(bf16[16,32,32]{2,1,0:T(8,128)(2,1)S(1)} %get-tuple-element.16, bf16[16,32,32]{2,1,0:T(8,128)(2,1)S(1)} %get-tuple-element.15, bf16[16,32,32]{2,1,0:T(8,128)(2,1)S(1)} %fusion.1), kind=kLoop, calls=%fused_computation.4 | loop fusion | flops 524288 | bytes 229376 | tf_op jit(solution)/shard_map/concatenate | solution.py:21
  13.9 5.3 %shard_map.73 = f32[2,16,128]{2,1,0:T(8,128)} custom-call(s32[2,384]{1,0:T(2,128)} %links, s32[2,384]{1,0:T(2,128)} %pairs.1, s32[2,64]{1,0:T(2,128)} %atoms.1, s32[2]{0:T(128)} %sizes.1, f32[1,2]{1,0:T(1,128)} %wts.1, s32[2,64]{1,0:T(2,128)} %convert_element_type.3.reach, bf16[4096,64]{1,0:T(8,128)(2,1)} %bitcast.24, bf16[1024,64]{1,0:T(8,128)(2,1)} %bitcast.27), custom_call_target="tpu_custom_call" | custom-call | tf_op jit(solution)/shard_map/pallas_call | solution.py:152
  19.2 1.6 %collective-permute-start.3 = (f32[2,16,128]{2,1,0:T(8,128)}, f32[2,16,128]{2,1,0:T(8,128)S(1)}, u32[]{:S(2)}, u32[]{:S(2)}) collective-permute-start(f32[2,16,128]{2,1,0:T(8,128)} %shard_map.73), channel_id=1, source_target_pairs={{0,8},{8,0},{16,24},{24,16},{1,9},{9,1},{17,25},{25,17},{2,10},{10... | collective-permute-start | bytes 49160 | tf_op jit(solution)/shard_map/ppermute | solution.py:136
  20.8 2.4 %collective-permute-done.3 = f32[2,16,128]{2,1,0:T(8,128)S(1)} collective-permute-done((f32[2,16,128]{2,1,0:T(8,128)}, f32[2,16,128]{2,1,0:T(8,128)S(1)}, u32[]{:S(2)}, u32[]{:S(2)}) %collective-permute-start.3) | collective-permute-done | bytes 16416 | tf_op jit(solution)/shard_map/ppermute | solution.py:136
  23.1 0.7 %add.6 = f32[2,16,128]{2,1,0:T(8,128)S(1)} add(f32[2,16,128]{2,1,0:T(8,128)} %shard_map.73, f32[2,16,128]{2,1,0:T(8,128)S(1)} %collective-permute-done.3) | non-fusion elementwise | flops 4096 | bytes 49152 | tf_op jit(solution)/shard_map/add | solution.py:136
  23.8 2.6 %collective-permute-start.4 = (f32[2,16,128]{2,1,0:T(8,128)S(1)}, f32[2,16,128]{2,1,0:T(8,128)S(1)}, u32[]{:S(2)}, u32[]{:S(2)}) collective-permute-start(f32[2,16,128]{2,1,0:T(8,128)S(1)} %add.6), channel_id=1, source_target_pairs={{0,16},{8,24},{16,0},{24,8},{1,17},{9,25},{17,1},{25,9},{2,18},{10... | collective-permute-start | bytes 49160 | tf_op jit(solution)/shard_map/ppermute | solution.py:136
  26.4 2.0 %collective-permute-done.4 = f32[2,16,128]{2,1,0:T(8,128)S(1)} collective-permute-done((f32[2,16,128]{2,1,0:T(8,128)S(1)}, f32[2,16,128]{2,1,0:T(8,128)S(1)}, u32[]{:S(2)}, u32[]{:S(2)}) %collective-permute-start.4) | collective-permute-done | bytes 16416 | tf_op jit(solution)/shard_map/ppermute | solution.py:136
  28.5 0.6 %copy.38 = f32[1,2,16,128]{3,1,2,0:T(2,128)} copy(f32[1,2,16,128]{3,2,1,0:T(8,128)S(1)} %add_bitcast_fusion) | data formatting | bytes 32768
  (12 shorter events, 0.3 us)
Async XLA Ops:
  0.0 1.5 %collective-permute-start = (bf16[1,2,2048]{2,1,0:T(2,128)(2,1)}, bf16[1,2,2048]{2,1,0:T(2,128)(2,1)S(1)}, u32[]{:S(2)}, u32[]{:S(2)}) collective-permute-start(bf16[1,2,2048]{2,1,0:T(2,128)(2,1)} %param.7), channel_id=1, source_target_pairs={{0,1},{1,0},{2,3},{3,2},{4,5},{5,4},{6,7},{7,6},{8,9},{9,8},{10,11... | collective-permute-start | bytes 24584 | tf_op jit(solution)/shard_map/ppermute | solution.py:120
  1.3 1.6 %copy-start = (bf16[1,2,2048]{2,1,0:T(2,128)(2,1)S(1)}, bf16[1,2,2048]{2,1,0:T(2,128)(2,1)}, u32[]{:S(2)}) copy-start(bf16[1,2,2048]{2,1,0:T(2,128)(2,1)} %param.7) | copy-start | bytes 24580
  3.0 5.7 %collective-permute-start.1 = (bf16[1,4,2048]{2,1,0:T(4,128)(2,1)S(1)}, bf16[1,4,2048]{2,1,0:T(4,128)(2,1)S(1)}, u32[]{:S(2)}, u32[]{:S(2)}) collective-permute-start(bf16[1,4,2048]{2,1,0:T(4,128)(2,1)S(1)} %maximum_select_fusion.3), channel_id=1, source_target_pairs={{0,2},{1,3},{2,0},{3,1},{4,6},{5,7},{6,4},{7,5},{8,10},{9,11},{10,... | collective-permute-start | bytes 49160 | tf_op jit(solution)/shard_map/ppermute | solution.py:120
  6.2 4.2 %copy-start.1 = (s32[2,384]{1,0:T(2,128)S(1)}, s32[2,384]{1,0:T(2,128)}, u32[]{:S(2)}) copy-start(s32[2,384]{1,0:T(2,128)} %links) | copy-start | bytes 9220
  8.8 4.0 %collective-permute-start.2 = (bf16[1,8,2048]{2,1,0:T(8,128)(2,1)S(1)}, bf16[1,8,2048]{2,1,0:T(8,128)(2,1)S(1)}, u32[]{:S(2)}, u32[]{:S(2)}) collective-permute-start(bf16[1,8,2048]{2,1,0:T(8,128)(2,1)S(1)} %maximum_select_fusion.2), channel_id=1, source_target_pairs={{0,4},{1,5},{2,6},{3,7},{4,0},{5,1},{6,2},{7,3},{8,12},{9,13},{10,... | collective-permute-start | bytes 98312 | tf_op jit(solution)/shard_map/ppermute | solution.py:120
  19.2 3.9 %collective-permute-start.3 = (f32[2,16,128]{2,1,0:T(8,128)}, f32[2,16,128]{2,1,0:T(8,128)S(1)}, u32[]{:S(2)}, u32[]{:S(2)}) collective-permute-start(f32[2,16,128]{2,1,0:T(8,128)} %shard_map.73), channel_id=1, source_target_pairs={{0,8},{8,0},{16,24},{24,16},{1,9},{9,1},{17,25},{25,17},{2,10},{10... | collective-permute-start | bytes 49160 | tf_op jit(solution)/shard_map/ppermute | solution.py:136
  23.8 4.6 %collective-permute-start.4 = (f32[2,16,128]{2,1,0:T(8,128)S(1)}, f32[2,16,128]{2,1,0:T(8,128)S(1)}, u32[]{:S(2)}, u32[]{:S(2)}) collective-permute-start(f32[2,16,128]{2,1,0:T(8,128)S(1)} %add.6), channel_id=1, source_target_pairs={{0,16},{8,24},{16,0},{24,8},{1,17},{9,25},{17,1},{25,9},{2,18},{10... | collective-permute-start | bytes 49160 | tf_op jit(solution)/shard_map/ppermute | solution.py:136

commit v2 on v1

--- a/solution.py
+++ b/solution.py
@@ -25,7 +25,7 @@
     a_dev = out.shape[0]
     zl = L * 2
     n1 = NB * NB
-    width = 4
+    width = 8
     spare = NB
 
     def rows(index):
@@ -159,7 +159,7 @@
             pltpu.VMEM((NB * 2 * L, L), jnp.bfloat16),
             pltpu.VMEM((2 * L, L), jnp.float32),
             pltpu.VMEM((NB + 1, 2 * L, L), jnp.float32),
-            pltpu.SMEM((4, NB * NB + 4), jnp.int32),
+            pltpu.SMEM((4, NB * NB + 8), jnp.int32),
         ],
     )(zone_link, pair_index, zone_atoms, zone_size, weights, reach, tab, tw)
     blocks = sum_energies(blocks, axis_sizes["energy"])

time: 29.2 us -> 29.2 us (level); the launches traced: 29.1 us -> 28.8 us
  Pallas kernels: 5.27 us -> 4.92 us
    pallas_call x1, Pallas kernels: 5.27 us -> 4.92 us  [body(): pl.pallas_call(zone_kernel, out_shape=jax.ShapeDtypeStruct((a_dev, 2 * L...]
where the time goes in v2:
time: 29.2 us; the launch traced here: 28.8 us
  starting transfers between devices  9.09 us (31%)
  waiting for transfers between devices  6.13 us (21%)
  local copies, waits for them, and re-layouts  5.55 us (19%)
  Pallas kernels  4.92 us (17%)
  other arithmetic  2.88 us (10%)
    ppermute x3, starting transfers between devices, gather_atoms(): other = lax.ppermute(blocks, 'atom', xor_pairs(n_axis, bit))  4.93 us
    pallas_call x1, Pallas kernels, body(): pl.pallas_call(zone_kernel, out_shape=jax.ShapeDtypeStruct((a_dev, 2 * L...  4.92 us
    ppermute x2, waiting for transfers between devices, sum_energies(): x = x + lax.ppermute(x, 'energy', xor_pairs(n_axis, bit))  4.43 us
    ppermute x2, starting transfers between devices, sum_energies(): x = x + lax.ppermute(x, 'energy', xor_pairs(n_axis, bit))  4.16 us
    concatenate x1, local copies, waits for them, and re-layouts, real_form(): return jnp.concatenate([top_rows, bottom_rows], axis=-2)  2.36 us
    ppermute x3, waiting for transfers between devices, gather_atoms(): other = lax.ppermute(blocks, 'atom', xor_pairs(n_axis, bit))  1.7 us
    optimization_barrier x1, local copies, waits for them, and re-layouts, gather_atoms(): other, later[bit - 1] = lax.optimization_barrier((other, later[bit - 1]))  1.22 us
    concatenate x2, other arithmetic, real_form(): return jnp.concatenate([top_rows, bottom_rows], axis=-2)  1.15 us
  transfers between devices with their start and end apart: 5, of which 4 were waited for; matrix products, arithmetic and copies ran while one was open for 15% of the time, Pallas kernels for 0%

profile of v2, /device:TPU:0, one launch (start us, length us, event | category | flops | bytes accessed | tf_op | source)
XLA Modules:
  0.0 28.8 jit_solution(214548912320259254)
XLA Ops:
  0.0 0.5 %collective-permute-start = (bf16[1,2,2048]{2,1,0:T(2,128)(2,1)}, bf16[1,2,2048]{2,1,0:T(2,128)(2,1)S(1)}, u32[]{:S(2)}, u32[]{:S(2)}) collective-permute-start(bf16[1,2,2048]{2,1,0:T(2,128)(2,1)} %param.7), channel_id=1, source_target_pairs={{0,1},{1,0},{2,3},{3,2},{4,5},{5,4},{6,7},{7,6},{8,9},{9,8},{10,11... | collective-permute-start | bytes 24584 | tf_op jit(solution)/shard_map/ppermute | solution.py:120
  0.5 0.8 %concatenate.135 = bf16[2,2,32,32]{3,2,1,0:T(8,128)(2,1)S(1)} reshape(bf16[1,2,2048]{2,1,0:T(2,128)(2,1)} %param.7) | data formatting | bytes 16384 | tf_op jit(solution)/shard_map/concatenate | solution.py:125
  1.3 0.0 copy-start
  1.3 0.2 collective-permute-done
  1.5 1.2 %copy.18 = bf16[1,64,2048]{1,2,0:T(8,128)(2,1)S(1)} copy(bf16[1,64,2048]{2,1,0:T(8,128)(2,1)} %param.8) | data formatting | bytes 524288 | tf_op jit(solution)/shard_map/optimization_barrier | solution.py:122
  2.8 0.1 concatenate.136
  2.9 0.0 copy-done
  3.0 2.9 %collective-permute-start.1 = (bf16[1,4,2048]{2,1,0:T(4,128)(2,1)S(1)}, bf16[1,4,2048]{2,1,0:T(4,128)(2,1)S(1)}, u32[]{:S(2)}, u32[]{:S(2)}) collective-permute-start(bf16[1,4,2048]{2,1,0:T(4,128)(2,1)S(1)} %maximum_select_fusion.3), channel_id=1, source_target_pairs={{0,2},{1,3},{2,0},{3,1},{4,6},{5,7},{6,4},{7,5},{8,10},{9,11},{10,... | collective-permute-start | bytes 49160 | tf_op jit(solution)/shard_map/ppermute | solution.py:120
  5.9 0.3 %maximum_maximum_fusion = bf16[64,64,64]{0,2,1:T(8,128)(2,1)S(1)} fusion(bf16[64,32,32]{0,2,1:T(8,128)(2,1)S(1)} %get-tuple-element.14, bf16[64,32,32]{0,2,1:T(8,128)(2,1)S(1)} %get-tuple-element.13, bf16[64,32,32]{0,2,1:T(8,128)(2,1)S(1)} %fusion.2), kind=kLoop, calls=%fused_computation | loop fusion | flops 2097152 | bytes 917504 | tf_op jit(solution)/shard_map/concatenate | solution.py:21
  6.2 0.0 copy-start.1
  6.2 2.4 %copy.19 = bf16[64,64,64]{2,1,0:T(8,128)(2,1)} copy(bf16[64,64,64]{0,2,1:T(8,128)(2,1)S(1)} %maximum_maximum_fusion) | data formatting | bytes 1048576 | tf_op jit(solution)/shard_map/concatenate | solution.py:21
  8.6 0.0 collective-permute-done.1
  8.6 0.1 concatenate.139
  8.8 1.6 %collective-permute-start.2 = (bf16[1,8,2048]{2,1,0:T(8,128)(2,1)S(1)}, bf16[1,8,2048]{2,1,0:T(8,128)(2,1)S(1)}, u32[]{:S(2)}, u32[]{:S(2)}) collective-permute-start(bf16[1,8,2048]{2,1,0:T(8,128)(2,1)S(1)} %maximum_select_fusion.2), channel_id=1, source_target_pairs={{0,4},{1,5},{2,6},{3,7},{4,0},{5,1},{6,2},{7,3},{8,12},{9,13},{10,... | collective-permute-start | bytes 98312 | tf_op jit(solution)/shard_map/ppermute | solution.py:120
  10.4 0.0 copy-done.1
  10.4 0.2 eq.21
  10.6 0.1 reduce_or.9
  10.7 0.6 %convert_element_type.3.reach = s32[2,64]{1,0:T(2,128)} convert(pred[2,64]{1,0:T(4,128)(4,1)S(1)} %reduce_or.9) | non-fusion elementwise | flops 128 | bytes 640 | tf_op jit(solution)/shard_map/convert_element_type | solution.py:149
  11.3 1.5 %collective-permute-done.2 = bf16[1,8,2048]{2,1,0:T(8,128)(2,1)S(1)} collective-permute-done((bf16[1,8,2048]{2,1,0:T(8,128)(2,1)S(1)}, bf16[1,8,2048]{2,1,0:T(8,128)(2,1)S(1)}, u32[]{:S(2)}, u32[]{:S(2)}) %collective-permute-start.2) | collective-permute-done | bytes 32800 | tf_op jit(solution)/shard_map/ppermute | solution.py:120
  12.7 0.1 concatenate.149
  12.9 0.1 maximum_select_fusion
  13.0 0.9 %maximum_maximum_fusion.1 = bf16[16,64,64]{2,1,0:T(8,128)(2,1)} fusion(bf16[16,32,32]{2,1,0:T(8,128)(2,1)S(1)} %get-tuple-element.16, bf16[16,32,32]{2,1,0:T(8,128)(2,1)S(1)} %get-tuple-element.15, bf16[16,32,32]{2,1,0:T(8,128)(2,1)S(1)} %fusion.1), kind=kLoop, calls=%fused_computation.4 | loop fusion | flops 524288 | bytes 229376 | tf_op jit(solution)/shard_map/concatenate | solution.py:21
  13.9 4.9 %shard_map.73 = f32[2,16,128]{2,1,0:T(8,128)} custom-call(s32[2,384]{1,0:T(2,128)} %links, s32[2,384]{1,0:T(2,128)} %pairs.1, s32[2,64]{1,0:T(2,128)} %atoms.1, s32[2]{0:T(128)} %sizes.1, f32[1,2]{1,0:T(1,128)} %wts.1, s32[2,64]{1,0:T(2,128)} %convert_element_type.3.reach, bf16[4096,64]{1,0:T(8,128)(2,1)} %bitcast.24, bf16[1024,64]{1,0:T(8,128)(2,1)} %bitcast.27), custom_call_target="tpu_custom_call" | custom-call | tf_op jit(solution)/shard_map/pallas_call | solution.py:152
  18.8 1.6 %collective-permute-start.3 = (f32[2,16,128]{2,1,0:T(8,128)}, f32[2,16,128]{2,1,0:T(8,128)S(1)}, u32[]{:S(2)}, u32[]{:S(2)}) collective-permute-start(f32[2,16,128]{2,1,0:T(8,128)} %shard_map.73), channel_id=1, source_target_pairs={{0,8},{8,0},{16,24},{24,16},{1,9},{9,1},{17,25},{25,17},{2,10},{10... | collective-permute-start | bytes 49160 | tf_op jit(solution)/shard_map/ppermute | solution.py:136
  20.4 2.4 %collective-permute-done.3 = f32[2,16,128]{2,1,0:T(8,128)S(1)} collective-permute-done((f32[2,16,128]{2,1,0:T(8,128)}, f32[2,16,128]{2,1,0:T(8,128)S(1)}, u32[]{:S(2)}, u32[]{:S(2)}) %collective-permute-start.3) | collective-permute-done | bytes 16416 | tf_op jit(solution)/shard_map/ppermute | solution.py:136
  22.8 0.7 %add.6 = f32[2,16,128]{2,1,0:T(8,128)S(1)} add(f32[2,16,128]{2,1,0:T(8,128)} %shard_map.73, f32[2,16,128]{2,1,0:T(8,128)S(1)} %collective-permute-done.3) | non-fusion elementwise | flops 4096 | bytes 49152 | tf_op jit(solution)/shard_map/add | solution.py:136
  23.5 2.6 %collective-permute-start.4 = (f32[2,16,128]{2,1,0:T(8,128)S(1)}, f32[2,16,128]{2,1,0:T(8,128)S(1)}, u32[]{:S(2)}, u32[]{:S(2)}) collective-permute-start(f32[2,16,128]{2,1,0:T(8,128)S(1)} %add.6), channel_id=1, source_target_pairs={{0,16},{8,24},{16,0},{24,8},{1,17},{9,25},{17,1},{25,9},{2,18},{10... | collective-permute-start | bytes 49160 | tf_op jit(solution)/shard_map/ppermute | solution.py:136
  26.1 2.1 %collective-permute-done.4 = f32[2,16,128]{2,1,0:T(8,128)S(1)} collective-permute-done((f32[2,16,128]{2,1,0:T(8,128)S(1)}, f32[2,16,128]{2,1,0:T(8,128)S(1)}, u32[]{:S(2)}, u32[]{:S(2)}) %collective-permute-start.4) | collective-permute-done | bytes 16416 | tf_op jit(solution)/shard_map/ppermute | solution.py:136
  28.1 0.6 %copy.38 = f32[1,2,16,128]{3,1,2,0:T(2,128)} copy(f32[1,2,16,128]{3,2,1,0:T(8,128)S(1)} %add_bitcast_fusion) | data formatting | bytes 32768
  (12 shorter events, 0.3 us)
Async XLA Ops:
  0.0 1.5 %collective-permute-start = (bf16[1,2,2048]{2,1,0:T(2,128)(2,1)}, bf16[1,2,2048]{2,1,0:T(2,128)(2,1)S(1)}, u32[]{:S(2)}, u32[]{:S(2)}) collective-permute-start(bf16[1,2,2048]{2,1,0:T(2,128)(2,1)} %param.7), channel_id=1, source_target_pairs={{0,1},{1,0},{2,3},{3,2},{4,5},{5,4},{6,7},{7,6},{8,9},{9,8},{10,11... | collective-permute-start | bytes 24584 | tf_op jit(solution)/shard_map/ppermute | solution.py:120
  1.3 1.6 %copy-start = (bf16[1,2,2048]{2,1,0:T(2,128)(2,1)S(1)}, bf16[1,2,2048]{2,1,0:T(2,128)(2,1)}, u32[]{:S(2)}) copy-start(bf16[1,2,2048]{2,1,0:T(2,128)(2,1)} %param.7) | copy-start | bytes 24580
  3.0 5.7 %collective-permute-start.1 = (bf16[1,4,2048]{2,1,0:T(4,128)(2,1)S(1)}, bf16[1,4,2048]{2,1,0:T(4,128)(2,1)S(1)}, u32[]{:S(2)}, u32[]{:S(2)}) collective-permute-start(bf16[1,4,2048]{2,1,0:T(4,128)(2,1)S(1)} %maximum_select_fusion.3), channel_id=1, source_target_pairs={{0,2},{1,3},{2,0},{3,1},{4,6},{5,7},{6,4},{7,5},{8,10},{9,11},{10,... | collective-permute-start | bytes 49160 | tf_op jit(solution)/shard_map/ppermute | solution.py:120
  6.2 4.2 %copy-start.1 = (s32[2,384]{1,0:T(2,128)S(1)}, s32[2,384]{1,0:T(2,128)}, u32[]{:S(2)}) copy-start(s32[2,384]{1,0:T(2,128)} %links) | copy-start | bytes 9220
  8.8 4.0 %collective-permute-start.2 = (bf16[1,8,2048]{2,1,0:T(8,128)(2,1)S(1)}, bf16[1,8,2048]{2,1,0:T(8,128)(2,1)S(1)}, u32[]{:S(2)}, u32[]{:S(2)}) collective-permute-start(bf16[1,8,2048]{2,1,0:T(8,128)(2,1)S(1)} %maximum_select_fusion.2), channel_id=1, source_target_pairs={{0,4},{1,5},{2,6},{3,7},{4,0},{5,1},{6,2},{7,3},{8,12},{9,13},{10,... | collective-permute-start | bytes 98312 | tf_op jit(solution)/shard_map/ppermute | solution.py:120
  18.8 3.9 %collective-permute-start.3 = (f32[2,16,128]{2,1,0:T(8,128)}, f32[2,16,128]{2,1,0:T(8,128)S(1)}, u32[]{:S(2)}, u32[]{:S(2)}) collective-permute-start(f32[2,16,128]{2,1,0:T(8,128)} %shard_map.73), channel_id=1, source_target_pairs={{0,8},{8,0},{16,24},{24,16},{1,9},{9,1},{17,25},{25,17},{2,10},{10... | collective-permute-start | bytes 49160 | tf_op jit(solution)/shard_map/ppermute | solution.py:136
  23.5 4.6 %collective-permute-start.4 = (f32[2,16,128]{2,1,0:T(8,128)S(1)}, f32[2,16,128]{2,1,0:T(8,128)S(1)}, u32[]{:S(2)}, u32[]{:S(2)}) collective-permute-start(f32[2,16,128]{2,1,0:T(8,128)S(1)} %add.6), channel_id=1, source_target_pairs={{0,16},{8,24},{16,0},{24,8},{1,17},{9,25},{17,1},{25,9},{2,18},{10... | collective-permute-start | bytes 49160 | tf_op jit(solution)/shard_map/ppermute | solution.py:136
